TPU v7x, 256 devices: a whole 4x4x8 slice. The times are simulated.
256 devices in a mesh: sec: 16 (over y, x), bulk: 16 (over z, core).
Axes of the slice: x: 4, y: 4, z: 8, core: 2. Of those that a mesh axis runs over, the one named last changes fastest.
Arguments:
- modes_x: bfloat16 [96, 16, 64, 8, 128], P(None, 'sec', 'bulk'), may hold values from -30 to 30
- modes_p: bfloat16 [96, 16, 64, 8, 128], P(None, 'sec', 'bulk'), may hold values from -30 to 30
- ritz_values: float32 [96], replicated, may hold values from 0.05 to 2
- node_types: int32 [16, 64, 8, 128], P('sec', 'bulk'), may hold values from 0 to 7
- stiff_table: float32 [8], replicated, may hold values from 1 to 10
- mass_table: float32 [8], replicated, may hold values from 0.5 to 4
- joint_nodes: int32 [16, 16, 16, 128], P('sec', 'bulk'), may hold values from 0 to 4095
- joint_count: int32 [16, 16, 16], P('sec', 'bulk'), may hold values from 0 to 128, as said below
Outputs:
- search_dir: bfloat16 [96, 16, 64, 8, 128], P(None, 'sec', 'bulk')
- ritz_pencil: float32 [288, 288], replicated
Inputs may be any that keep to these rules, and one draw needn't show every extreme that they name: `joint_nodes`: local node numbers of a slab; slots at or beyond the count are ignored; a node may appear in several slots. Symmetric: joint_count[a, b, c] = joint_count[c, b, a], zero for a = c.
All inputs are finite; a program needn't handle non-finite values.
Results may differ from a plain program's by a relative error of at most 0.0004.
The roundings to bfloat16 on the way count: a program that leaves them out, or rounds other values in their place, can miss the bound.
Values may be sent and summed in bfloat16 or wider, within the bound.
No kernel may reach another device: no remote copies, remote signals or barrier semaphores. Data moves between devices by JAX's collectives and lax.ppermute only.
A program may use at most 64 MiB of HBM per device.

v0:
```python
import jax
import jax.numpy as jnp
from jax import lax
from jax.sharding import PartitionSpec as P

JOINT_GAIN = 0.5
SPRING = (0.0, 0.1, 0.05, 0.025)
OFFSETS = [
    (step_z, step_y, step_x)
    for step_z in (-1, 0, 1)
    for step_y in (-1, 0, 1)
    for step_x in (-1, 0, 1)
    if (step_z, step_y, step_x) != (0, 0, 0)
]


def extended(shard, sides, width):
    for axis, dim in sides:
        peers, length = (lax.axis_size(axis), shard.shape[dim])
        up = [(i, (i + 1) % peers) for i in range(peers - 1)]
        down = [(j, i) for i, j in up]
        last = lax.slice_in_dim(shard, length - width, length, axis=dim)
        first = lax.slice_in_dim(shard, 0, width, axis=dim)
        before = lax.ppermute(last, axis, up)
        after = lax.ppermute(first, axis, down)
        shard = jnp.concatenate([before, shard, after], axis=dim)
    return shard


def lower_solve(lower, matrix):
    return lax.linalg.triangular_solve(lower, matrix, left_side=True, lower=True)


def edge_weights(kappa_pad):
    padded = jnp.pad(kappa_pad.astype(jnp.float32), ((0, 0), (1, 1), (1, 1)))
    depth = padded.shape[0] - 2
    height = padded.shape[1] - 2
    breadth = padded.shape[2] - 2
    centre = padded[1:-1, 1:-1, 1:-1]
    weights = []
    summed = jnp.zeros(centre.shape, jnp.float32)
    for offset in OFFSETS:
        step_z, step_y, step_x = offset
        other = padded[
            1 + step_z : 1 + step_z + depth,
            1 + step_y : 1 + step_y + height,
            1 + step_x : 1 + step_x + breadth,
        ]
        reach = abs(step_z) + abs(step_y) + abs(step_x)
        weight = SPRING[reach] * 2.0 * centre * other / (centre + other)
        weights.append(weight)
        summed = summed + weight
    return (weights, summed)


def apply_stencil(values_pad, weights, summed):
    padded = jnp.pad(values_pad, ((0, 0), (0, 0), (1, 1), (1, 1)))
    depth = padded.shape[1] - 2
    height = padded.shape[2] - 2
    breadth = padded.shape[3] - 2
    accum = jnp.zeros((padded.shape[0], depth, height, breadth), jnp.float32)
    for offset, weight in zip(OFFSETS, weights):
        step_z, step_y, step_x = offset
        other = padded[
            :,
            1 + step_z : 1 + step_z + depth,
            1 + step_y : 1 + step_y + height,
            1 + step_x : 1 + step_x + breadth,
        ]
        accum = accum + weight[None] * other.astype(jnp.float32)
    centre = padded[:, 1:-1, 1:-1, 1:-1].astype(jnp.float32)
    return summed[None] * centre - accum


def joint_apply(result, sent, recv, node_ids, joint_w):
    width = result.shape[0]
    delta = joint_w.reshape(1, -1) * (sent.astype(jnp.float32) - recv.astype(jnp.float32)).reshape(
        width, -1
    )
    return result.reshape(width, -1).at[:, node_ids].add(delta).reshape(result.shape)


def mirror(matrix):
    return jnp.triu(matrix) + jnp.transpose(jnp.triu(matrix, 1))


def fetch(block, node_ids, sections, capacity):
    padded = extended(block, (("bulk", 1),), 1)
    width = block.shape[0]
    sent = jnp.take(block.reshape(width, -1), node_ids, axis=1).reshape(width, sections, capacity)
    recv = lax.all_to_all(sent, "sec", split_axis=1, concat_axis=1, tiled=True)
    return (padded, sent, recv)


def on_device(
    modes_x, modes_p, ritz_values, node_types, stiff_table, mass_table, joint_nodes, joint_count
):
    modes = modes_x.shape[0]
    sections = joint_nodes.shape[2]
    capacity = joint_nodes.shape[3]
    columns = 3 * modes
    levels = jnp.arange(stiff_table.shape[0], dtype=jnp.int32)[:, None, None, None]
    chosen = node_types[0][None] == levels
    kappa = jnp.sum(jnp.where(chosen, stiff_table[:, None, None, None], 0.0), axis=0).astype(
        jnp.bfloat16
    )
    mass = jnp.sum(jnp.where(chosen, mass_table[:, None, None, None], 0.0), axis=0)
    node_ids = joint_nodes[0, 0].reshape(-1)
    live = (jnp.arange(capacity, dtype=jnp.int32)[None, :] < joint_count[0, 0][:, None]).astype(
        jnp.float32
    )
    x_local = modes_x[:, 0]
    p_local = modes_p[:, 0]
    k_row = x_local.shape[0]
    first = jnp.concatenate([x_local, kappa[None]], axis=0)
    padded, sent, recv = fetch(first, node_ids, sections, capacity)
    weights, summed = edge_weights(padded[k_row])
    own = sent[k_row].astype(jnp.float32)
    other = recv[k_row].astype(jnp.float32)
    joint_w = JOINT_GAIN * 2.0 * own * other / (own + other) * live
    diag_full = summed.reshape(-1).at[node_ids].add(joint_w.reshape(-1)).reshape(summed.shape)
    stiff_first = joint_apply(
        apply_stencil(padded[:k_row], weights, summed),
        sent[:k_row],
        recv[:k_row],
        node_ids,
        joint_w,
    )
    resid = (
        stiff_first - mass[None] * x_local.astype(jnp.float32) * ritz_values[:, None, None, None]
    )
    search_local = (resid / diag_full[None]).astype(jnp.bfloat16)
    second = jnp.concatenate([search_local, p_local], axis=0)
    padded_two, sent_two, recv_two = fetch(second, node_ids, sections, capacity)
    stiff_wp = joint_apply(
        apply_stencil(padded_two, weights, summed), sent_two, recv_two, node_ids, joint_w
    )
    span = jnp.concatenate([x_local, second], axis=0).reshape(columns, -1)
    stiff_span = (
        jnp.concatenate([stiff_first, stiff_wp], axis=0).astype(jnp.bfloat16).reshape(columns, -1)
    )
    mass_span = (mass.reshape(1, -1) * span.astype(jnp.float32)).astype(jnp.bfloat16)
    contract = (((1,), (1,)), ((), ()))
    gram_k = lax.dot_general(span, stiff_span, contract, preferred_element_type=jnp.float32)
    gram_m = lax.dot_general(span, mass_span, contract, preferred_element_type=jnp.float32)
    summed_grams = lax.psum((mirror(gram_k), mirror(gram_m)), ("sec", "bulk"))
    stiff_gram = summed_grams[0]
    mass_gram = summed_grams[1]
    lower = jnp.linalg.cholesky(mass_gram)
    half = lower_solve(lower, stiff_gram)
    ritz_pencil = lower_solve(lower, jnp.transpose(half))
    return (search_local[:, None], ritz_pencil)


def solution(mesh):
    placed = (
        P(None, "sec", "bulk", None, None),
        P(None, "sec", "bulk", None, None),
        P(),
        P("sec", "bulk", None, None),
        P(),
        P(),
        P("sec", "bulk", None, None),
        P("sec", "bulk", None),
    )
    return jax.shard_map(
        on_device,
        mesh=mesh,
        in_specs=placed,
        out_specs=(P(None, "sec", "bulk", None, None), P()),
        check_vma=False,
    )
```

profile of v0, /device:TPU:1, one launch (start us, length us, event | category | flops | bytes accessed | tf_op | source)
XLA Modules:
  0.0 561.0 jit_solution(11046337085348744172)
XLA Ops:
  7.2 0.8 select_reduce_fusion
  8.0 2.9 copy_bitcast_fusion
  10.9 0.8 pad_maximum_fusion.13
  11.7 5.1 collective-permute-start.1
  16.8 1.9 collective-permute-start
  18.8 3.2 convert_element_type.349
  21.9 0.8 copy.195
  22.9 2.1 pad_maximum_fusion.6
  25.0 6.2 %gather_fusion = bf16[2048,97]{1,0:T(8,128)(2,1)S(1)} fusion(bf16[97,4096]{0,1:T(8,128)(2,1)S(1)} %pad_maximum_fusion.6, s32[2048]{0:T(1024)S(1)} %broadcast_clamp_fusion), kind=kCustom, calls=%fused_computation | custom fusion | bytes 802816 | tf_op jit(solution)/shard_map/jit(_take)/gather | solution.py:90
  31.5 0.8 broadcast_select_fusion.1
  32.3 6.6 %all-to-all-start = ((bf16[97,16,128]{2,0,1:T(8,128)(2,1)}), bf16[97,16,128]{2,0,1:T(8,128)(2,1)}, u32[]{:S(2)}, u32[]{:S(2)}) async-start(bf16[97,16,128]{2,0,1:T(8,128)(2,1)} %broadcast_select_fusion.1), calls=%async_computation | async-start | bytes 851968 | tf_op jit(solution)/shard_map/all_to_all | solution.py:91
  39.0 1.6 copy.207
  41.1 1.4 bitcast_select_fusion
  42.6 1.1 copy.243
  43.7 1.1 copy.202
  46.6 3.3 select_maximum_fusion.2
  50.2 9.1 %fusion.32 = f32[96,4,8,128]{3,0,2,1:T(8,128)} fusion(bf16[96,4,8,128]{3,0,2,1:T(8,128)(2,1)S(1)} %get-tuple-element.94, bf16[96,6,10,130]{3,0,2,1:T(8,128)(2,1)S(1)} %select_maximum_fusion.2, bf16[97,1,8,128]{3,0,2,1:T(8,128)(2,1)} %collective-permute-done.1, bf16[1,4,8,128]{3,0,2,1:T(2,128)(2,1)S(1)} %copy.191, ...), kind=kLoop, calls=%fused_computation.62 | loop fusion | flops 35389440 | bytes 22081536 | tf_op jit(solution)/shard_map/sub | solution.py:72
  59.3 1.8 copy.232
  61.2 0.8 slice.545
  62.0 1.4 copy.199
  63.4 2.7 convert_reduce_fusion
  66.0 2.0 fusion.46
  68.1 2.5 copy.205
  70.7 12.8 %scatter_fusion = f32[96,4096]{0,1:T(8,128)S(1)} fusion(f32[96,4096]{0,1:T(8,128)S(1)} %bitcast.245, s32[2048]{0:T(1024)S(1)} %bitcast.263, f32[2048,96]{1,0:T(8,128)} %copy.205), kind=kCustom, calls=%fused_computation.2 | custom fusion | flops 196608 | bytes 2367488 | tf_op jit(solution)/shard_map/scatter-add | solution.py:80
  83.4 1.7 copy.211
  85.2 11.5 %scatter_fusion.1 = f32[4096]{0:T(1024)S(1)} fusion(f32[4096]{0:T(1024)S(1)} %copy.258, s32[2048]{0:T(1024)S(1)} %bitcast.264, f32[2048]{0:T(1024)S(1)} %fusion.79), kind=kCustom, calls=%fused_computation.3 | custom fusion | flops 2048 | bytes 32768 | tf_op jit(solution)/shard_map/scatter-add | solution.py:121
  96.7 3.7 divide_convert_fusion
  100.5 1.5 fusion.87
  101.9 1.1 fusion.50
  103.1 1.9 collective-permute-start.3
  105.0 3.6 collective-permute-start.2
  108.6 4.1 fusion.11
  112.8 2.2 pad_maximum_fusion
  115.0 1.9 copy.206
  116.9 1.0 copy.208
  117.8 10.3 %gather_fusion.1 = bf16[2048,192]{1,0:T(8,128)(2,1)} fusion(bf16[192,4096]{0,1:T(8,128)(2,1)} %pad_maximum_fusion, s32[2048]{0:T(1024)S(1)} %copy-done.75), kind=kCustom, calls=%fused_computation.1 | custom fusion | bytes 1581056 | tf_op jit(solution)/shard_map/jit(_take)/gather | solution.py:90
  128.1 1.7 copy.215
  129.9 1.0 broadcast_select_fusion
  130.8 6.7 %all-to-all-start.1 = ((bf16[192,16,128]{2,0,1:T(8,128)(2,1)}), bf16[192,16,128]{2,0,1:T(8,128)(2,1)}, u32[]{:S(2)}, u32[]{:S(2)}) async-start(bf16[192,16,128]{2,0,1:T(8,128)(2,1)} %broadcast_select_fusion), calls=%async_computation.1 | async-start | bytes 1572864 | tf_op jit(solution)/shard_map/all_to_all | solution.py:91
  138.1 5.7 %select_maximum_fusion = bf16[192,6,10,130]{3,0,2,1:T(8,128)(2,1)S(1)} fusion(bf16[192,1,8,128]{3,0,2,1:T(8,128)(2,1)} %collective-permute-done.3, bf16[192,1,8,128]{3,0,2,1:T(8,128)(2,1)} %collective-permute-done.2, bf16[96,4,8,128]{3,0,2,1:T(8,128)(2,1)S(1)} %copy-done.4, bf16[96,4,8,128]{3,0,2,1:T(8,128)(2,1)S(1)} %copy-done.6), kind=kLoop, calls=%fused_computation.19 | loop fusion | flops 34444800 | bytes 5354496 | tf_op jit(solution)/shard_map/concatenate | solution.py:26
  144.1 17.5 %add_subtract_fusion = f32[192,4,8,128]{3,0,2,1:T(8,128)} fusion(bf16[96,4,8,128]{3,0,2,1:T(8,128)(2,1)S(1)} %copy-done.4, bf16[96,4,8,128]{3,0,2,1:T(8,128)(2,1)S(1)} %copy-done.6, bf16[192,6,10,130]{3,0,2,1:T(8,128)(2,1)S(1)} %select_maximum_fusion, bf16[192,1,8,128]{3,0,2,1:T(8,128)(2,1)} %collective-permute-done.3, ...), kind=kLoop, calls=%fused_computation.35 | loop fusion | flops 73138176 | bytes 43696128 | tf_op jit(solution)/shard_map/sub | solution.py:72
  161.5 4.9 copy.236
  166.5 2.5 fusion.36
  169.0 2.8 copy.218
  171.9 16.1 %scatter_fusion.2 = f32[192,4096]{0,1:T(8,128)} fusion(f32[192,4096]{0,1:T(8,128)} %bitcast.244, s32[2048]{0:T(1024)S(1)} %bitcast.265, f32[2048,192]{1,0:T(8,128)} %copy.218), kind=kCustom, calls=%fused_computation.4 | custom fusion | flops 393216 | bytes 4726784 | tf_op jit(solution)/shard_map/scatter-add | solution.py:80
  187.9 4.8 copy.219
  192.8 1.7 copy.244
  195.7 2.2 fusion.38
  197.9 2.1 copy.221
  200.0 2.2 fusion.49
  202.2 1.2 divide_convert_fusion.1
  203.5 258.2 %all-reduce.9.cloned.1.call-done = (f32[288,288]{1,0:T(8,128)}, f32[288,288]{1,0:T(8,128)}) async-done(((f32[288,288]{1,0:T(8,128)}, f32[288,288]{1,0:T(8,128)}), (f32[288,288]{1,0:T(8,128)}, f32[288,288]{1,0:T(8,128)})) %all-reduce.9.cloned.1.call-update) | async-done | bytes 663568 | tf_op jit(solution)/shard_map/psum | solution.py:146
  461.7 1.3 copy.209
  463.0 1.1 fusion.48
  464.1 11.7 %cholesky.77 = f32[128,128]{1,0:T(8,128)S(1)} custom-call(f32[128,128]{1,0:T(8,128)S(1)} %cholesky.195), custom_call_target="Cholesky" | custom-call | tf_op jit(solution)/shard_map/jit(cholesky)/cholesky | solution.py:149
  475.9 9.8 %custom-call.22 = f32[1,128,128]{1,2,0:T(8,128)S(1)} custom-call(f32[1,128,128]{2,1,0:T(8,128)S(1)} %get-tuple-element.86), custom_call_target="InvertDiagBlocksLowerTriangular" | custom-call | tf_op jit(solution)/shard_map/jit(cholesky)/cholesky | solution.py:149
  486.2 11.9 %cholesky.162 = f32[128,128]{1,0:T(8,128)S(1)} custom-call(f32[128,128]{1,0:T(8,128)S(1)} %cholesky.199), custom_call_target="Cholesky" | custom-call | tf_op jit(solution)/shard_map/jit(cholesky)/cholesky | solution.py:149
  498.1 9.8 %custom-call.23 = f32[1,128,128]{1,2,0:T(8,128)S(1)} custom-call(f32[1,128,128]{2,1,0:T(8,128)S(1)} %get-tuple-element.83), custom_call_target="InvertDiagBlocksLowerTriangular" | custom-call | tf_op jit(solution)/shard_map/jit(cholesky)/cholesky | solution.py:149
  508.2 2.9 cholesky.184
  515.2 4.0 while.4
  515.8 1.4 bitcast_dynamic-update-slice_fusion.2
  517.8 1.4 bitcast_dynamic-update-slice_fusion.2
  519.3 29.5 %custom-call.26 = f32[3,128,128]{1,2,0:T(8,128)S(1)} custom-call(f32[3,128,128]{2,1,0:T(8,128)S(1)} %pad_maximum_fusion.14), custom_call_target="InvertDiagBlocksLowerTriangular" | custom-call | tf_op jit(solution)/shard_map/triangular_solve/custom-call.2 | solution.py:31
  553.0 1.0 copy.226
  (234 shorter events, 12.9 us)
Async XLA Ops:
  8.0 13.9 %copy-start = (bf16[96,1,4,8,128]{4,3,2,1,0:T(8,128)(2,1)S(1)}, bf16[96,1,4,8,128]{4,3,2,1,0:T(8,128)(2,1)}, u32[]{:S(2)}) copy-start(bf16[96,1,4,8,128]{4,3,2,1,0:T(8,128)(2,1)} %param.10) | copy-start | bytes 2359300
  10.9 11.8 %copy-start.73 = (s32[1,1,16,128]{3,2,1,0:T(8,128)S(1)}, s32[1,1,16,128]{3,2,1,0:T(8,128)}, u32[]{:S(2)}) copy-start(s32[1,1,16,128]{3,2,1,0:T(8,128)} %param.16) | copy-start | bytes 24580
  11.7 33.7 %collective-permute-start.1 = (bf16[97,1,8,128]{3,0,2,1:T(8,128)(2,1)}, bf16[97,1,8,128]{3,0,2,1:T(8,128)(2,1)}, u32[]{:S(2)}, u32[]{:S(2)}) collective-permute-start(bf16[97,1,8,128]{3,0,2,1:T(8,128)(2,1)} %get-tuple-element.81), channel_id=1, source_target_pairs={{1,0},{2,1},{3,2},{4,3},{5,4},{6,5},{7,6},{8,7},{9,8},{10,9},{11,1... | collective-permute-start | bytes 595976 | tf_op jit(solution)/shard_map/ppermute | solution.py:25
  16.8 28.6 %collective-permute-start = (bf16[97,1,8,128]{3,0,2,1:T(8,128)(2,1)}, bf16[97,1,8,128]{3,0,2,1:T(8,128)(2,1)}, u32[]{:S(2)}, u32[]{:S(2)}) collective-permute-start(bf16[97,1,8,128]{3,0,2,1:T(8,128)(2,1)} %get-tuple-element.80), channel_id=1, source_target_pairs={{0,1},{1,2},{2,3},{3,4},{4,5},{5,6},{6,7},{7,8},{8,9},{9,10},{10,1... | collective-permute-start | bytes 595976 | tf_op jit(solution)/shard_map/ppermute | solution.py:24
  22.8 8.4 %copy-start.7 = (bf16[96,1,4,8,128]{0,4,3,2,1:T(8,128)(2,1)}, bf16[96,1,4,8,128]{0,4,3,2,1:T(8,128)(2,1)S(1)}, u32[]{:S(2)}) copy-start(bf16[96,1,4,8,128]{0,4,3,2,1:T(8,128)(2,1)S(1)} %copy.195) | copy-start | bytes 2359300
  22.8 8.7 %copy-start.77 = (pred[16,128]{1,0:T(8,128)(4,1)}, pred[16,128]{1,0:T(8,128)(4,1)S(1)}, u32[]{:S(2)}) copy-start(pred[16,128]{1,0:T(8,128)(4,1)S(1)} %compare_and_fusion) | copy-start | bytes 6148
  22.8 8.3 %copy-start.74 = (s32[2048]{0:T(1024)}, s32[2048]{0:T(1024)S(1)}, u32[]{:S(2)}) copy-start(s32[2048]{0:T(1024)S(1)} %broadcast_clamp_fusion) | copy-start | bytes 24580
  31.2 9.9 %copy-start.12 = (bf16[2048,97]{1,0:T(8,128)(2,1)}, bf16[2048,97]{1,0:T(8,128)(2,1)S(1)}, u32[]{:S(2)}) copy-start(bf16[2048,97]{1,0:T(8,128)(2,1)S(1)} %gather_fusion) | copy-start | bytes 1191940
  31.2 7.8 %copy-start.13 = (bf16[96,1,4,8,128]{4,3,2,1,0:T(8,128)(2,1)S(1)}, bf16[96,1,4,8,128]{4,3,2,1,0:T(8,128)(2,1)}, u32[]{:S(2)}) copy-start(bf16[96,1,4,8,128]{4,3,2,1,0:T(8,128)(2,1)} %param.11) | copy-start | bytes 2359300
  31.5 11.0 %copy-start.83 = (s32[1,1,16]{2,1,0:T(1,128)S(1)}, s32[1,1,16]{2,1,0:T(1,128)}, u32[]{:S(2)}) copy-start(s32[1,1,16]{2,1,0:T(1,128)} %param.17) | copy-start | bytes 196
  32.3 28.8 %all-to-all-start = ((bf16[97,16,128]{2,0,1:T(8,128)(2,1)}), bf16[97,16,128]{2,0,1:T(8,128)(2,1)}, u32[]{:S(2)}, u32[]{:S(2)}) async-start(bf16[97,16,128]{2,0,1:T(8,128)(2,1)} %broadcast_select_fusion.1), calls=%async_computation | async-start | bytes 851968 | tf_op jit(solution)/shard_map/all_to_all | solution.py:91
  46.4 3.5 copy-start.20
  46.4 3.5 copy-start.22
  66.0 4.5 copy-start.76
  66.0 4.5 copy-start.84
  85.1 11.5 %copy-start.81 = (f32[96]{0:T(128)S(1)}, f32[96]{0:T(128)}, u32[]{:S(2)}) copy-start(f32[96]{0:T(128)} %param.12) | copy-start | bytes 1156
  96.7 3.8 copy-start.1
  96.7 3.8 copy-start.10
  100.4 8.2 %copy-start.8 = (bf16[96,1,4,8,128]{0,4,3,2,1:T(8,128)(2,1)S(1)}, bf16[96,1,4,8,128]{0,4,3,2,1:T(8,128)(2,1)}, u32[]{:S(2)}) copy-start(bf16[96,1,4,8,128]{0,4,3,2,1:T(8,128)(2,1)} %copy-done.7) | copy-start | bytes 2359300
  100.4 8.2 %copy-start.11 = (bf16[96,1,4,8,128]{0,4,3,2,1:T(8,128)(2,1)S(1)}, bf16[96,1,4,8,128]{0,4,3,2,1:T(8,128)(2,1)}, u32[]{:S(2)}) copy-start(bf16[96,1,4,8,128]{0,4,3,2,1:T(8,128)(2,1)} %copy.207) | copy-start | bytes 2359300
  103.1 35.0 %collective-permute-start.3 = (bf16[192,1,8,128]{3,0,2,1:T(8,128)(2,1)}, bf16[192,1,8,128]{3,0,2,1:T(8,128)(2,1)}, u32[]{:S(2)}, u32[]{:S(2)}) collective-permute-start(bf16[192,1,8,128]{3,0,2,1:T(8,128)(2,1)} %get-tuple-element.79), channel_id=1, source_target_pairs={{1,0},{2,1},{3,2},{4,3},{5,4},{6,5},{7,6},{8,7},{9,8},{10,9},{11,1... | collective-permute-start | bytes 1179656 | tf_op jit(solution)/shard_map/ppermute | solution.py:25
  105.0 33.1 %collective-permute-start.2 = (bf16[192,1,8,128]{3,0,2,1:T(8,128)(2,1)}, bf16[192,1,8,128]{3,0,2,1:T(8,128)(2,1)}, u32[]{:S(2)}, u32[]{:S(2)}) collective-permute-start(bf16[192,1,8,128]{3,0,2,1:T(8,128)(2,1)} %get-tuple-element.78), channel_id=1, source_target_pairs={{0,1},{1,2},{2,3},{3,4},{4,5},{5,6},{6,7},{7,8},{8,9},{9,10},{10,1... | collective-permute-start | bytes 1179656 | tf_op jit(solution)/shard_map/ppermute | solution.py:24
  112.7 4.1 copy-start.15
  117.8 12.0 %copy-start.78 = (pred[16,128]{1,0:T(8,128)(4,1)S(1)}, pred[16,128]{1,0:T(8,128)(4,1)}, u32[]{:S(2)}) copy-start(pred[16,128]{1,0:T(8,128)(4,1)} %copy-done.77) | copy-start | bytes 6148
  128.1 9.9 %copy-start.4 = (bf16[96,4,8,128]{3,0,2,1:T(8,128)(2,1)S(1)}, bf16[96,4,8,128]{3,0,2,1:T(8,128)(2,1)}, u32[]{:S(2)}) copy-start(bf16[96,4,8,128]{3,0,2,1:T(8,128)(2,1)} %get-tuple-element.93) | copy-start | bytes 2359300
  128.1 9.9 %copy-start.6 = (bf16[96,4,8,128]{3,0,2,1:T(8,128)(2,1)S(1)}, bf16[96,4,8,128]{3,0,2,1:T(8,128)(2,1)}, u32[]{:S(2)}) copy-start(bf16[96,4,8,128]{3,0,2,1:T(8,128)(2,1)} %copy-done.5) | copy-start | bytes 2359300
  130.8 35.6 %all-to-all-start.1 = ((bf16[192,16,128]{2,0,1:T(8,128)(2,1)}), bf16[192,16,128]{2,0,1:T(8,128)(2,1)}, u32[]{:S(2)}, u32[]{:S(2)}) async-start(bf16[192,16,128]{2,0,1:T(8,128)(2,1)} %broadcast_select_fusion), calls=%async_computation.1 | async-start | bytes 1572864 | tf_op jit(solution)/shard_map/all_to_all | solution.py:91
  137.5 6.3 %copy-start.21 = (f32[4,8,128]{2,1,0:T(8,128)S(1)}, f32[4,8,128]{2,1,0:T(8,128)}, u32[]{:S(2)}) copy-start(f32[4,8,128]{2,1,0:T(8,128)} %copy-done.20) | copy-start | bytes 49156
  137.5 6.3 %copy-start.23 = (f32[4,8,128]{2,1,0:T(8,128)S(1)}, f32[4,8,128]{2,1,0:T(8,128)}, u32[]{:S(2)}) copy-start(f32[4,8,128]{2,1,0:T(8,128)} %copy-done.22) | copy-start | bytes 49156
  137.5 6.3 %copy-start.25 = (f32[4,8,128]{2,1,0:T(8,128)S(1)}, f32[4,8,128]{2,1,0:T(8,128)}, u32[]{:S(2)}) copy-start(f32[4,8,128]{2,1,0:T(8,128)} %copy-done.24) | copy-start | bytes 49156
  137.5 6.3 %copy-start.27 = (f32[4,8,128]{2,1,0:T(8,128)S(1)}, f32[4,8,128]{2,1,0:T(8,128)}, u32[]{:S(2)}) copy-start(f32[4,8,128]{2,1,0:T(8,128)} %copy-done.26) | copy-start | bytes 49156
  137.6 6.3 %copy-start.29 = (f32[4,8,128]{2,1,0:T(8,128)S(1)}, f32[4,8,128]{2,1,0:T(8,128)}, u32[]{:S(2)}) copy-start(f32[4,8,128]{2,1,0:T(8,128)} %copy-done.28) | copy-start | bytes 49156
  137.6 6.3 %copy-start.31 = (f32[4,8,128]{2,1,0:T(8,128)S(1)}, f32[4,8,128]{2,1,0:T(8,128)}, u32[]{:S(2)}) copy-start(f32[4,8,128]{2,1,0:T(8,128)} %copy-done.30) | copy-start | bytes 49156
  137.6 6.3 %copy-start.33 = (f32[4,8,128]{2,1,0:T(8,128)S(1)}, f32[4,8,128]{2,1,0:T(8,128)}, u32[]{:S(2)}) copy-start(f32[4,8,128]{2,1,0:T(8,128)} %copy-done.32) | copy-start | bytes 49156
  137.6 6.3 %copy-start.35 = (f32[4,8,128]{2,1,0:T(8,128)S(1)}, f32[4,8,128]{2,1,0:T(8,128)}, u32[]{:S(2)}) copy-start(f32[4,8,128]{2,1,0:T(8,128)} %copy-done.34) | copy-start | bytes 49156
  137.6 6.3 %copy-start.37 = (f32[4,8,128]{2,1,0:T(8,128)S(1)}, f32[4,8,128]{2,1,0:T(8,128)}, u32[]{:S(2)}) copy-start(f32[4,8,128]{2,1,0:T(8,128)} %copy-done.36) | copy-start | bytes 49156
  137.6 6.3 %copy-start.39 = (f32[4,8,128]{2,1,0:T(8,128)S(1)}, f32[4,8,128]{2,1,0:T(8,128)}, u32[]{:S(2)}) copy-start(f32[4,8,128]{2,1,0:T(8,128)} %copy-done.38) | copy-start | bytes 49156
  137.6 6.3 %copy-start.41 = (f32[4,8,128]{2,1,0:T(8,128)S(1)}, f32[4,8,128]{2,1,0:T(8,128)}, u32[]{:S(2)}) copy-start(f32[4,8,128]{2,1,0:T(8,128)} %copy-done.40) | copy-start | bytes 49156
  137.6 6.3 %copy-start.43 = (f32[4,8,128]{2,1,0:T(8,128)S(1)}, f32[4,8,128]{2,1,0:T(8,128)}, u32[]{:S(2)}) copy-start(f32[4,8,128]{2,1,0:T(8,128)} %copy-done.42) | copy-start | bytes 49156
  137.6 6.3 %copy-start.45 = (f32[4,8,128]{2,1,0:T(8,128)S(1)}, f32[4,8,128]{2,1,0:T(8,128)}, u32[]{:S(2)}) copy-start(f32[4,8,128]{2,1,0:T(8,128)} %copy-done.44) | copy-start | bytes 49156
  137.6 6.3 %copy-start.47 = (f32[4,8,128]{2,1,0:T(8,128)S(1)}, f32[4,8,128]{2,1,0:T(8,128)}, u32[]{:S(2)}) copy-start(f32[4,8,128]{2,1,0:T(8,128)} %copy-done.46) | copy-start | bytes 49156
  137.7 6.3 %copy-start.49 = (f32[4,8,128]{2,1,0:T(8,128)S(1)}, f32[4,8,128]{2,1,0:T(8,128)}, u32[]{:S(2)}) copy-start(f32[4,8,128]{2,1,0:T(8,128)} %copy-done.48) | copy-start | bytes 49156
  137.7 6.3 %copy-start.51 = (f32[4,8,128]{2,1,0:T(8,128)S(1)}, f32[4,8,128]{2,1,0:T(8,128)}, u32[]{:S(2)}) copy-start(f32[4,8,128]{2,1,0:T(8,128)} %copy-done.50) | copy-start | bytes 49156
  137.7 6.3 %copy-start.53 = (f32[4,8,128]{2,1,0:T(8,128)S(1)}, f32[4,8,128]{2,1,0:T(8,128)}, u32[]{:S(2)}) copy-start(f32[4,8,128]{2,1,0:T(8,128)} %copy-done.52) | copy-start | bytes 49156
  137.7 324.0 %all-reduce.9.cloned.1.call-start = ((), (), s32[]{:S(2)}) async-start(), calls=%async_computation.2 | async-start | bytes 1769472 | tf_op jit(solution)/shard_map/psum | solution.py:146
  137.9 6.0 %copy-start.55 = (f32[4,8,128]{2,1,0:T(8,128)S(1)}, f32[4,8,128]{2,1,0:T(8,128)}, u32[]{:S(2)}) copy-start(f32[4,8,128]{2,1,0:T(8,128)} %copy-done.54) | copy-start | bytes 49156
  138.0 6.0 %copy-start.57 = (f32[4,8,128]{2,1,0:T(8,128)S(1)}, f32[4,8,128]{2,1,0:T(8,128)}, u32[]{:S(2)}) copy-start(f32[4,8,128]{2,1,0:T(8,128)} %copy-done.56) | copy-start | bytes 49156
  138.0 6.0 %copy-start.59 = (f32[4,8,128]{2,1,0:T(8,128)S(1)}, f32[4,8,128]{2,1,0:T(8,128)}, u32[]{:S(2)}) copy-start(f32[4,8,128]{2,1,0:T(8,128)} %copy-done.58) | copy-start | bytes 49156
  138.0 6.0 %copy-start.61 = (f32[4,8,128]{2,1,0:T(8,128)S(1)}, f32[4,8,128]{2,1,0:T(8,128)}, u32[]{:S(2)}) copy-start(f32[4,8,128]{2,1,0:T(8,128)} %copy-done.60) | copy-start | bytes 49156
  138.0 6.0 %copy-start.63 = (f32[4,8,128]{2,1,0:T(8,128)S(1)}, f32[4,8,128]{2,1,0:T(8,128)}, u32[]{:S(2)}) copy-start(f32[4,8,128]{2,1,0:T(8,128)} %copy-done.62) | copy-start | bytes 49156
  138.0 6.0 %copy-start.65 = (f32[4,8,128]{2,1,0:T(8,128)S(1)}, f32[4,8,128]{2,1,0:T(8,128)}, u32[]{:S(2)}) copy-start(f32[4,8,128]{2,1,0:T(8,128)} %copy-done.64) | copy-start | bytes 49156
  138.0 6.0 %copy-start.67 = (f32[4,8,128]{2,1,0:T(8,128)S(1)}, f32[4,8,128]{2,1,0:T(8,128)}, u32[]{:S(2)}) copy-start(f32[4,8,128]{2,1,0:T(8,128)} %copy-done.66) | copy-start | bytes 49156
  138.0 6.0 %copy-start.69 = (f32[4,8,128]{2,1,0:T(8,128)S(1)}, f32[4,8,128]{2,1,0:T(8,128)}, u32[]{:S(2)}) copy-start(f32[4,8,128]{2,1,0:T(8,128)} %copy-done.68) | copy-start | bytes 49156
  138.0 6.0 %copy-start.71 = (f32[4,8,128]{2,1,0:T(8,128)S(1)}, f32[4,8,128]{2,1,0:T(8,128)}, u32[]{:S(2)}) copy-start(f32[4,8,128]{2,1,0:T(8,128)} %copy-done.70) | copy-start | bytes 49156
  161.5 4.9 copy-start.79
  195.7 4.3 copy-start.16
  195.7 4.3 copy-start.17
  195.7 4.3 copy-start.80
  197.8 4.4 copy-start.2
  197.9 4.4 copy-start.9
  197.9 4.4 copy-start.82
  461.7 53.4 %copy-start.85 = (s32[2]{0:T(128)S(1)}, s32[2]{0:T(128)}, u32[]{:S(2)}) copy-start(s32[2]{0:T(128)} %iota_multiply_fusion) | copy-start | bytes 28
  461.7 53.5 %copy-start.72 = (f32[2,128,128]{2,1,0:T(8,128)S(1)}, f32[2,128,128]{2,1,0:T(8,128)}, u32[]{:S(2)}) copy-start(f32[2,128,128]{2,1,0:T(8,128)} %custom-call.31) | copy-start | bytes 393220
  464.0 84.8 %copy-start.19 = (f32[288,288]{1,0:T(8,128)S(1)}, f32[288,288]{1,0:T(8,128)}, u32[]{:S(2)}) copy-start(f32[288,288]{1,0:T(8,128)} %get-tuple-element.45) | copy-start | bytes 995332
  (29 other events, 94.4 us)
Sparse Core Ops, SparseCore 0:
  202.3 259.3 all-reduce.8
where the time goes:
time: 570 us; the launch traced here: 561 us
  waiting for transfers between devices  258 us (45%)
  other arithmetic  183 us (32%)
  local copies, waits for them, and re-layouts  64.5 us (11%)
  starting transfers between devices  26.1 us (5%)
  between operations  17.7 us (3%)
  matrix products  11.1 us (2%)
    psum x1, waiting for transfers between devices, on_device(): summed_grams = lax.psum((mirror(gram_k), mirror(gram_m)), ('sec', 'bulk'))  258 us
    another operation x11, other arithmetic, on_device(): lower = jnp.linalg.cholesky(mass_gram)  48.2 us
    another operation x9, other arithmetic, lower_solve(): lax.linalg.triangular_solve(lower, matrix, left_side=True, lower=True)  30.3 us
    scatter-add x2, other arithmetic, joint_apply(): result.reshape(width, -1).at[:, node_ids].add(delta).reshape(result.shape)  28.9 us
    sub x2, other arithmetic, apply_stencil(): return summed[None] * centre - accum  26.6 us
    gather x4, local copies, waits for them, and re-layouts, fetch(): jnp.take(block.reshape(width, -1), node_ids, axis=1)  18.5 us
    all_to_all x2, starting transfers between devices, fetch(): recv = lax.all_to_all(sent, 'sec', split_axis=1, concat_axis=1, tiled=True)  13.3 us
    scatter-add x1, other arithmetic, on_device(): summed.reshape(-1).at[node_ids].add(joint_w.reshape(-1))  11.5 us
  transfers between devices with their start and end apart: 7, of which 1 were waited for; matrix products, arithmetic and copies ran while one was open for 15% of the time, Pallas kernels for 0%

commit v1 on v0

--- a/solution.py
+++ b/solution.py
@@ -80,6 +80,34 @@
     return result.reshape(width, -1).at[:, node_ids].add(delta).reshape(result.shape)
 
 
+def upper_blocks(rows, cols, width):
+    contract = (((1,), (1,)), ((), ()))
+    parts = []
+    for index in range(rows.shape[0] // width):
+        part = lax.dot_general(
+            rows[index * width : (index + 1) * width],
+            cols[index * width :],
+            contract,
+            preferred_element_type=jnp.float32,
+        )
+        parts.append(part)
+    return jnp.concatenate(parts, axis=1)
+
+
+def unpack_blocks(packed, width):
+    blocks = 0
+    while width * blocks * (blocks + 1) // 2 < packed.shape[1]:
+        blocks += 1
+    offset = 0
+    rows = []
+    for index in range(blocks):
+        span = (blocks - index) * width
+        gap = jnp.zeros((width, index * width), packed.dtype)
+        rows.append(jnp.concatenate([gap, packed[:, offset : offset + span]], axis=1))
+        offset += span
+    return jnp.concatenate(rows, axis=0)
+
+
 def mirror(matrix):
     return jnp.triu(matrix) + jnp.transpose(jnp.triu(matrix, 1))
 
@@ -140,15 +168,17 @@
         jnp.concatenate([stiff_first, stiff_wp], axis=0).astype(jnp.bfloat16).reshape(columns, -1)
     )
     mass_span = (mass.reshape(1, -1) * span.astype(jnp.float32)).astype(jnp.bfloat16)
-    contract = (((1,), (1,)), ((), ()))
-    gram_k = lax.dot_general(span, stiff_span, contract, preferred_element_type=jnp.float32)
-    gram_m = lax.dot_general(span, mass_span, contract, preferred_element_type=jnp.float32)
-    summed_grams = lax.psum((mirror(gram_k), mirror(gram_m)), ("sec", "bulk"))
-    stiff_gram = summed_grams[0]
-    mass_gram = summed_grams[1]
+    gram_m = lax.psum(lax.psum(upper_blocks(span, mass_span, modes), "bulk"), "sec")
+    stiff_part = upper_blocks(span, stiff_span, modes)
+    gram_m, stiff_part = lax.optimization_barrier((gram_m, stiff_part))
+    gram_k = lax.psum(lax.psum(stiff_part, "bulk"), "sec")
+    mass_gram = mirror(unpack_blocks(gram_m, modes))
+    stiff_gram = mirror(unpack_blocks(gram_k, modes))
     lower = jnp.linalg.cholesky(mass_gram)
-    half = lower_solve(lower, stiff_gram)
-    ritz_pencil = lower_solve(lower, jnp.transpose(half))
+    inverse = lower_solve(lower, jnp.eye(columns, dtype=jnp.float32))
+    exact = lax.Precision.HIGHEST
+    half = jnp.matmul(inverse, stiff_gram, precision=exact)
+    ritz_pencil = jnp.matmul(half, jnp.transpose(inverse), precision=exact)
     return (search_local[:, None], ritz_pencil)
 
 

time: 570 us -> 570 us (level)
  other arithmetic: 183 us -> 220 us
  waiting for transfers between devices: 258 us -> 225 us
  local copies, waits for them, and re-layouts: 64.5 us -> 56 us
    psum x1 -> x4, waiting for transfers between devices: 258 us -> 225 us  [the longest x2 116 us: on_device(): gram_k = lax.psum(lax.psum(stiff_part, 'bulk'), 'sec')]
    concatenate x2, other arithmetic: 9 us -> 25.2 us  [extended(): shard = jnp.concatenate([before, shard, after], axis=dim)]
    sub x2, other arithmetic: 26.6 us -> 38.4 us  [apply_stencil(): return summed[None] * centre - accum]
    reshape x5 -> x2, local copies, waits for them, and re-layouts: 10.9 us -> 3.71 us  [joint_apply(): result.reshape(width, -1).at[:, node_ids].add(delta).reshape(result.shape)]
    sub x0 -> x2, local copies, waits for them, and re-layouts: none -> 6.96 us  [apply_stencil(): return summed[None] * centre - accum]
    dot_general x2 -> x8, matrix products: 6.25 us -> 12.7 us  [the longest x6 9 us: upper_blocks(): lax.dot_general(rows[index * width:(index + 1) * width], cols[index * wid...]
    another operation x9 -> x7, other arithmetic: 30.3 us -> 30.8 us  [lower_solve(): lax.linalg.triangular_solve(lower, matrix, left_side=True, lower=True)]
    another operation x11 -> x10, other arithmetic: 48.2 us -> 47.7 us  [on_device(): lower = jnp.linalg.cholesky(mass_gram)]
  transfers between devices with their start and end apart: 7 -> 10, of which waited for: 1 -> 4; matrix products, arithmetic and copies ran while one was open for 15% -> 40% of each run, Pallas kernels for 0% -> 0%
where the time goes in v1:
time: 570 us; the launch traced here: 561 us
  waiting for transfers between devices  225 us (39%)
  other arithmetic  220 us (39%)
  local copies, waits for them, and re-layouts  56 us (10%)
  starting transfers between devices  26.4 us (5%)
  between operations  17.7 us (3%)
  matrix products  16 us (3%)
    psum x2, waiting for transfers between devices, on_device(): gram_k = lax.psum(lax.psum(stiff_part, 'bulk'), 'sec')  116 us
    psum x1, waiting for transfers between devices, on_device(): lax.psum(upper_blocks(span, mass_span, modes), 'bulk')  90.3 us
    another operation x10, other arithmetic, on_device(): lower = jnp.linalg.cholesky(mass_gram)  47.7 us
    sub x2, other arithmetic, apply_stencil(): return summed[None] * centre - accum  38.4 us
    another operation x7, other arithmetic, lower_solve(): lax.linalg.triangular_solve(lower, matrix, left_side=True, lower=True)  30.8 us
    scatter-add x2, other arithmetic, joint_apply(): result.reshape(width, -1).at[:, node_ids].add(delta).reshape(result.shape)  29.2 us
    concatenate x2, other arithmetic, extended(): shard = jnp.concatenate([before, shard, after], axis=dim)  25.2 us
    gather x4, local copies, waits for them, and re-layouts, fetch(): jnp.take(block.reshape(width, -1), node_ids, axis=1)  18.6 us
  transfers between devices with their start and end apart: 10, of which 4 were waited for; matrix products, arithmetic and copies ran while one was open for 40% of the time, Pallas kernels for 0%

profile of v1, /device:TPU:1, one launch (start us, length us, event | category | flops | bytes accessed | tf_op | source)
XLA Modules:
  0.0 560.5 jit_solution(6228942137165287355)
XLA Ops:
  8.1 1.8 pad_maximum_fusion.17
  9.9 5.1 collective-permute-start.1
  15.0 1.9 collective-permute-start
  16.9 3.2 convert_element_type.358
  21.0 2.1 pad_maximum_fusion.6
  23.1 6.2 %gather_fusion = bf16[2048,97]{1,0:T(8,128)(2,1)S(1)} fusion(bf16[97,4096]{0,1:T(8,128)(2,1)S(1)} %pad_maximum_fusion.6, s32[2048]{0:T(1024)S(1)} %broadcast_clamp_fusion), kind=kCustom, calls=%fused_computation | custom fusion | bytes 802816 | tf_op jit(solution)/shard_map/jit(_take)/gather | solution.py:118
  30.5 6.6 %all-to-all-start = ((bf16[97,16,128]{2,0,1:T(8,128)(2,1)}), bf16[97,16,128]{2,0,1:T(8,128)(2,1)}, u32[]{:S(2)}, u32[]{:S(2)}) async-start(bf16[97,16,128]{2,0,1:T(8,128)(2,1)} %broadcast_select_fusion.1), calls=%async_computation | async-start | bytes 851968 | tf_op jit(solution)/shard_map/all_to_all | solution.py:119
  38.5 1.4 bitcast_select_fusion
  40.0 1.1 copy.215
  41.1 1.1 copy.163
  42.2 1.6 copy.167
  46.8 8.7 %select_maximum_fusion.2 = bf16[96,6,10,130]{3,2,1,0:T(8,128)(2,1)S(1)} fusion(bf16[97,1,8,128]{3,2,1,0:T(8,128)(2,1)} %collective-permute-done.1, bf16[97,1,8,128]{3,2,1,0:T(8,128)(2,1)} %collective-permute-done, bf16[1,4,8,128]{3,2,1,0:T(8,128)(2,1)S(1)} %bitcast.263, bf16[96,4,8,128]{3,2,1,0:T(8,128)(2,1)S(1)} %bitcast.241), kind=kLoop, calls=%fused_computation.29 | loop fusion | flops 17222400 | bytes 2689536 | tf_op jit(solution)/shard_map/concatenate | solution.py:26
  55.8 11.2 %fusion.22 = f32[96,4,8,128]{3,2,1,0:T(8,128)} fusion(bf16[96,4,8,128]{3,2,1,0:T(8,128)(2,1)S(1)} %bitcast.242, bf16[96,6,10,130]{3,2,1,0:T(8,128)(2,1)S(1)} %select_maximum_fusion.2, bf16[97,1,8,128]{3,2,1,0:T(8,128)(2,1)} %collective-permute-done.1, bf16[1,4,8,128]{3,2,1,0:T(8,128)(2,1)S(1)} %bitcast.264, bf16[97,1,8,128]{3,2,1,0:T(8,128)(2,1)} %collective-permute-done, ...), kind=kLoop, calls=%fused_computation.52 | loop fusion | flops 33030144 | bytes 22081536 | tf_op jit(solution)/shard_map/sub | solution.py:72
  67.0 1.9 copy.155
  69.6 1.4 copy.160
  71.0 2.1 convert_reduce_fusion
  73.1 2.0 fusion.36
  75.1 2.4 copy.165
  77.6 13.1 %scatter_fusion = f32[96,4096]{0,1:T(8,128)S(1)} fusion(f32[96,4096]{0,1:T(8,128)S(1)} %bitcast.236, s32[2048]{0:T(1024)S(1)} %bitcast.267, f32[2048,96]{1,0:T(8,128)} %copy.165), kind=kCustom, calls=%fused_computation.2 | custom fusion | flops 196608 | bytes 2367488 | tf_op jit(solution)/shard_map/scatter-add | solution.py:80
  90.7 11.5 %scatter_fusion.1 = f32[4096]{0:T(1024)S(1)} fusion(f32[4096]{0:T(1024)S(1)} %copy.227, s32[2048]{0:T(1024)S(1)} %bitcast.268, f32[2048]{0:T(1024)S(1)} %fusion.69), kind=kCustom, calls=%fused_computation.3 | custom fusion | flops 2048 | bytes 32768 | tf_op jit(solution)/shard_map/scatter-add | solution.py:149
  102.3 4.6 fusion.78
  106.8 2.6 multiply_convert_fusion
  109.4 1.8 fusion.20
  111.2 1.3 convolution_bitcast_fusion
  112.5 2.2 pad_maximum_fusion
  114.7 1.8 copy.166
  116.6 1.9 copy.168
  118.4 2.8 divide_convert_fusion.1
  122.5 1.0 fusion.44
  123.4 1.9 collective-permute-start.3
  125.4 3.6 collective-permute-start.2
  129.0 2.3 convolution_bitcast_fusion.3
  132.3 9.8 %gather_fusion.1 = bf16[2048,192]{1,0:T(8,128)(2,1)} fusion(bf16[192,4096]{0,1:T(8,128)(2,1)S(1)} %copy-done.1, s32[2048]{0:T(1024)} %copy-done.80), kind=kCustom, calls=%fused_computation.1 | custom fusion | bytes 1581056 | tf_op jit(solution)/shard_map/jit(_take)/gather | solution.py:118
  142.0 2.4 copy.170
  144.4 2.1 broadcast_select_fusion
  146.6 6.6 %all-to-all-start.1 = ((bf16[192,16,128]{2,0,1:T(8,128)(2,1)}), bf16[192,16,128]{2,0,1:T(8,128)(2,1)}, u32[]{:S(2)}, u32[]{:S(2)}) async-start(bf16[192,16,128]{2,0,1:T(8,128)(2,1)} %broadcast_select_fusion), calls=%async_computation.1 | async-start | bytes 1572864 | tf_op jit(solution)/shard_map/all_to_all | solution.py:119
  153.3 90.3 %all-reduce.15.cloned.1.call-done = f32[96,576]{1,0:T(8,128)} async-done(((f32[96,576]{1,0:T(8,128)}), f32[96,576]{1,0:T(8,128)}) %all-reduce.15.cloned.1.call-update) | async-done | bytes 221200 | tf_op jit(solution)/shard_map/psum | solution.py:171
  244.1 16.5 %select_maximum_fusion = bf16[192,6,10,130]{3,2,1,0:T(8,128)(2,1)S(1)} fusion(bf16[192,1,8,128]{3,2,1,0:T(8,128)(2,1)S(1)} %collective-permute-done.3, bf16[192,1,8,128]{3,2,1,0:T(8,128)(2,1)} %collective-permute-done.2, bf16[96,4,8,128]{3,2,1,0:T(8,128)(2,1)S(1)} %bitcast.253, bf16[96,4,8,128]{3,2,1,0:T(8,128)(2,1)S(1)} %copy-done.3), kind=kLoop, calls=%fused_computation.18 | loop fusion | flops 34444800 | bytes 5354496 | tf_op jit(solution)/shard_map/concatenate | solution.py:26
  260.9 27.3 %add_subtract_fusion = f32[192,4,8,128]{3,2,1,0:T(8,128)} fusion(bf16[96,4,8,128]{3,2,1,0:T(8,128)(2,1)S(1)} %bitcast.254, bf16[96,4,8,128]{3,2,1,0:T(8,128)(2,1)S(1)} %copy-done.3, bf16[192,6,10,130]{3,2,1,0:T(8,128)(2,1)S(1)} %select_maximum_fusion, bf16[192,1,8,128]{3,2,1,0:T(8,128)(2,1)S(1)} %collective-permute-done.3, ...), kind=kLoop, calls=%fused_computation.40 | loop fusion | flops 66846720 | bytes 43696128 | tf_op jit(solution)/shard_map/sub | solution.py:72
  288.2 5.1 copy.169
  293.3 2.6 fusion.26
  295.9 2.8 copy.172
  298.8 16.1 %scatter_fusion.2 = f32[192,4096]{0,1:T(8,128)} fusion(f32[192,4096]{0,1:T(8,128)} %bitcast.235, s32[2048]{0:T(1024)S(1)} %bitcast.269, f32[2048,192]{1,0:T(8,128)} %copy.172), kind=kCustom, calls=%fused_computation.4 | custom fusion | flops 393216 | bytes 4726784 | tf_op jit(solution)/shard_map/scatter-add | solution.py:80
  314.9 2.5 convert.18
  318.2 1.9 fusion.28
  321.8 18.4 %all-reduce.17.cloned.1.call-done = f32[96,576]{1,0:T(8,128)} async-done(((f32[96,576]{1,0:T(8,128)}), f32[96,576]{1,0:T(8,128)}) %all-reduce.17.cloned.1.call-update) | async-done | bytes 221200 | tf_op jit(solution)/shard_map/psum | solution.py:171
  340.2 1.0 slice.510
  341.2 1.0 slice.509
  342.2 0.9 slice.508
  344.2 11.7 %cholesky.77 = f32[128,128]{1,0:T(8,128)S(1)} custom-call(f32[128,128]{1,0:T(8,128)S(1)} %copy.181), custom_call_target="Cholesky" | custom-call | tf_op jit(solution)/shard_map/jit(cholesky)/cholesky | solution.py:177
  356.0 9.8 %custom-call.22 = f32[1,128,128]{1,2,0:T(8,128)S(1)} custom-call(f32[1,128,128]{2,1,0:T(8,128)S(1)} %get-tuple-element.65), custom_call_target="InvertDiagBlocksLowerTriangular" | custom-call | tf_op jit(solution)/shard_map/jit(cholesky)/cholesky | solution.py:177
  366.6 11.7 %cholesky.162 = f32[128,128]{1,0:T(8,128)S(1)} custom-call(f32[128,128]{1,0:T(8,128)S(1)} %copy.183), custom_call_target="Cholesky" | custom-call | tf_op jit(solution)/shard_map/jit(cholesky)/cholesky | solution.py:177
  378.4 10.0 %custom-call.23 = f32[1,128,128]{1,2,0:T(8,128)S(1)} custom-call(f32[1,128,128]{2,1,0:T(8,128)S(1)} %get-tuple-element.62), custom_call_target="InvertDiagBlocksLowerTriangular" | custom-call | tf_op jit(solution)/shard_map/jit(cholesky)/cholesky | solution.py:177
  388.9 2.9 cholesky.184
  395.2 3.9 while.1
  395.9 1.3 bitcast_dynamic-update-slice_fusion.2
  397.8 1.3 bitcast_dynamic-update-slice_fusion.2
  399.2 29.5 %custom-call.24 = f32[3,128,128]{1,2,0:T(8,128)S(1)} custom-call(f32[3,128,128]{2,1,0:T(8,128)S(1)} %pad_maximum_fusion.18), custom_call_target="InvertDiagBlocksLowerTriangular" | custom-call | tf_op jit(solution)/shard_map/triangular_solve | solution.py:31
  428.8 1.0 fusion.53
  430.7 20.5 %all-reduce.19.cloned.1.call-done = f32[96,576]{0,1:T(8,128)} async-done(((f32[96,576]{0,1:T(8,128)}), f32[96,576]{0,1:T(8,128)}) %all-reduce.19.cloned.1.call-update) | async-done | bytes 221200 | tf_op jit(solution)/shard_map/psum | solution.py:174
  451.5 95.4 %all-reduce.21.cloned.1.call-done = f32[96,576]{0,1:T(8,128)} async-done(((f32[96,576]{0,1:T(8,128)}), f32[96,576]{0,1:T(8,128)}) %all-reduce.21.cloned.1.call-update) | async-done | bytes 221200 | tf_op jit(solution)/shard_map/psum | solution.py:174
  548.6 0.9 slice.591
  549.8 2.0 fusion.38
  551.8 1.8 fusion.46
  (255 shorter events, 21.7 us)
Async XLA Ops:
  7.2 12.9 %copy-start = (bf16[96,1,4,8,128]{4,3,2,1,0:T(8,128)(2,1)S(1)}, bf16[96,1,4,8,128]{4,3,2,1,0:T(8,128)(2,1)}, u32[]{:S(2)}) copy-start(bf16[96,1,4,8,128]{4,3,2,1,0:T(8,128)(2,1)} %param.8) | copy-start | bytes 2359300
  7.2 13.7 %copy-start.79 = (s32[1,1,16,128]{3,2,1,0:T(8,128)S(1)}, s32[1,1,16,128]{3,2,1,0:T(8,128)}, u32[]{:S(2)}) copy-start(s32[1,1,16,128]{3,2,1,0:T(8,128)} %param.14) | copy-start | bytes 24580
  9.9 35.8 %collective-permute-start.1 = (bf16[97,1,8,128]{3,2,1,0:T(8,128)(2,1)}, bf16[97,1,8,128]{3,2,1,0:T(8,128)(2,1)}, u32[]{:S(2)}, u32[]{:S(2)}) collective-permute-start(bf16[97,1,8,128]{3,2,1,0:T(8,128)(2,1)} %get-tuple-element.60), channel_id=1, source_target_pairs={{1,0},{2,1},{3,2},{4,3},{5,4},{6,5},{7,6},{8,7},{9,8},{10,9},{11,1... | collective-permute-start | bytes 595976 | tf_op jit(solution)/shard_map/ppermute | solution.py:25
  15.0 30.7 %collective-permute-start = (bf16[97,1,8,128]{3,2,1,0:T(8,128)(2,1)}, bf16[97,1,8,128]{3,2,1,0:T(8,128)(2,1)}, u32[]{:S(2)}, u32[]{:S(2)}) collective-permute-start(bf16[97,1,8,128]{3,2,1,0:T(8,128)(2,1)} %get-tuple-element.59), channel_id=1, source_target_pairs={{0,1},{1,2},{2,3},{3,4},{4,5},{5,6},{6,7},{7,8},{8,9},{9,10},{10,1... | collective-permute-start | bytes 595976 | tf_op jit(solution)/shard_map/ppermute | solution.py:24
  21.0 69.7 %copy-start.21 = (s32[2048,1]{0,1:T(1,128)}, s32[2048,1]{0,1:T(1,128)S(1)}, u32[]{:S(2)}) copy-start(s32[2048,1]{0,1:T(1,128)S(1)} %compare_select_fusion) | copy-start | bytes 24580
  29.3 9.1 %copy-start.15 = (bf16[2048,97]{1,0:T(8,128)(2,1)}, bf16[2048,97]{1,0:T(8,128)(2,1)S(1)}, u32[]{:S(2)}) copy-start(bf16[2048,97]{1,0:T(8,128)(2,1)S(1)} %gather_fusion) | copy-start | bytes 1191940
  29.4 10.5 %copy-start.85 = (s32[1,1,16]{2,1,0:T(1,128)S(1)}, s32[1,1,16]{2,1,0:T(1,128)}, u32[]{:S(2)}) copy-start(s32[1,1,16]{2,1,0:T(1,128)} %param.15) | copy-start | bytes 196
  29.7 12.5 %copy-start.9 = (bf16[96,1,4,8,128]{4,3,2,1,0:T(8,128)(2,1)S(1)}, bf16[96,1,4,8,128]{4,3,2,1,0:T(8,128)(2,1)}, u32[]{:S(2)}) copy-start(bf16[96,1,4,8,128]{4,3,2,1,0:T(8,128)(2,1)} %param.9) | copy-start | bytes 2359300
  30.5 38.3 %all-to-all-start = ((bf16[97,16,128]{2,0,1:T(8,128)(2,1)}), bf16[97,16,128]{2,0,1:T(8,128)(2,1)}, u32[]{:S(2)}, u32[]{:S(2)}) async-start(bf16[97,16,128]{2,0,1:T(8,128)(2,1)} %broadcast_select_fusion.1), calls=%async_computation | async-start | bytes 851968 | tf_op jit(solution)/shard_map/all_to_all | solution.py:119
  37.1 206.5 %all-reduce.15.cloned.1.call-start = ((), (), s32[]{:S(2)}) async-start(), calls=%async_computation.2 | async-start | bytes 491520 | tf_op jit(solution)/shard_map/psum | solution.py:171
  46.6 8.9 %copy-start.23 = (f32[4,8,128]{2,1,0:T(8,128)}, f32[4,8,128]{2,1,0:T(8,128)S(1)}, u32[]{:S(2)}) copy-start(f32[4,8,128]{2,1,0:T(8,128)S(1)} %get-tuple-element.27) | copy-start | bytes 49156
  46.6 8.9 %copy-start.25 = (f32[4,8,128]{2,1,0:T(8,128)}, f32[4,8,128]{2,1,0:T(8,128)S(1)}, u32[]{:S(2)}) copy-start(f32[4,8,128]{2,1,0:T(8,128)S(1)} %get-tuple-element.28) | copy-start | bytes 49156
  46.6 8.9 %copy-start.27 = (f32[4,8,128]{2,1,0:T(8,128)}, f32[4,8,128]{2,1,0:T(8,128)S(1)}, u32[]{:S(2)}) copy-start(f32[4,8,128]{2,1,0:T(8,128)S(1)} %get-tuple-element.29) | copy-start | bytes 49156
  46.6 8.9 %copy-start.29 = (f32[4,8,128]{2,1,0:T(8,128)}, f32[4,8,128]{2,1,0:T(8,128)S(1)}, u32[]{:S(2)}) copy-start(f32[4,8,128]{2,1,0:T(8,128)S(1)} %get-tuple-element.30) | copy-start | bytes 49156
  46.6 8.9 %copy-start.31 = (f32[4,8,128]{2,1,0:T(8,128)}, f32[4,8,128]{2,1,0:T(8,128)S(1)}, u32[]{:S(2)}) copy-start(f32[4,8,128]{2,1,0:T(8,128)S(1)} %get-tuple-element.31) | copy-start | bytes 49156
  46.6 8.9 %copy-start.33 = (f32[4,8,128]{2,1,0:T(8,128)}, f32[4,8,128]{2,1,0:T(8,128)S(1)}, u32[]{:S(2)}) copy-start(f32[4,8,128]{2,1,0:T(8,128)S(1)} %get-tuple-element.32) | copy-start | bytes 49156
  46.6 8.9 %copy-start.35 = (f32[4,8,128]{2,1,0:T(8,128)}, f32[4,8,128]{2,1,0:T(8,128)S(1)}, u32[]{:S(2)}) copy-start(f32[4,8,128]{2,1,0:T(8,128)S(1)} %get-tuple-element.33) | copy-start | bytes 49156
  46.7 8.9 %copy-start.37 = (f32[4,8,128]{2,1,0:T(8,128)}, f32[4,8,128]{2,1,0:T(8,128)S(1)}, u32[]{:S(2)}) copy-start(f32[4,8,128]{2,1,0:T(8,128)S(1)} %get-tuple-element.34) | copy-start | bytes 49156
  46.7 8.9 %copy-start.39 = (f32[4,8,128]{2,1,0:T(8,128)}, f32[4,8,128]{2,1,0:T(8,128)S(1)}, u32[]{:S(2)}) copy-start(f32[4,8,128]{2,1,0:T(8,128)S(1)} %get-tuple-element.35) | copy-start | bytes 49156
  46.7 8.9 %copy-start.41 = (f32[4,8,128]{2,1,0:T(8,128)}, f32[4,8,128]{2,1,0:T(8,128)S(1)}, u32[]{:S(2)}) copy-start(f32[4,8,128]{2,1,0:T(8,128)S(1)} %get-tuple-element.36) | copy-start | bytes 49156
  73.1 17.6 %copy-start.77 = (f32[2048]{0:T(1024)}, f32[2048]{0:T(1024)S(1)}, u32[]{:S(2)}) copy-start(f32[2048]{0:T(1024)S(1)} %get-tuple-element.15) | copy-start | bytes 24580
  90.7 11.5 %copy-start.84 = (f32[96]{0:T(128)S(1)}, f32[96]{0:T(128)}, u32[]{:S(2)}) copy-start(f32[96]{0:T(128)} %param.10) | copy-start | bytes 1156
  121.6 9.8 %copy-start.19 = (f32[96,192]{1,0:T(8,128)S(1)}, f32[96,192]{1,0:T(8,128)}, u32[]{:S(2)}) copy-start(f32[96,192]{1,0:T(8,128)} %fusion.20) | copy-start | bytes 221188
  121.6 9.8 %copy-start.75 = (f32[96,288]{1,0:T(8,128)S(1)}, f32[96,288]{1,0:T(8,128)}, u32[]{:S(2)}) copy-start(f32[96,288]{1,0:T(8,128)} %convolution_bitcast_fusion) | copy-start | bytes 331780
  122.5 9.8 %copy-start.1 = (bf16[192,4096]{0,1:T(8,128)(2,1)S(1)}, bf16[192,4096]{0,1:T(8,128)(2,1)}, u32[]{:S(2)}) copy-start(bf16[192,4096]{0,1:T(8,128)(2,1)} %pad_maximum_fusion) | copy-start | bytes 4718596
  123.4 120.7 %collective-permute-start.3 = (bf16[192,1,8,128]{3,2,1,0:T(8,128)(2,1)}, bf16[192,1,8,128]{3,2,1,0:T(8,128)(2,1)S(1)}, u32[]{:S(2)}, u32[]{:S(2)}) collective-permute-start(bf16[192,1,8,128]{3,2,1,0:T(8,128)(2,1)} %get-tuple-element.58), channel_id=1, source_target_pairs={{1,0},{2,1},{3,2},{4,3},{5,4},{6,5},{7,6},{8,7},{9,8},{10,9},{11,1... | collective-permute-start | bytes 1179656 | tf_op jit(solution)/shard_map/ppermute | solution.py:25
  125.4 118.8 %collective-permute-start.2 = (bf16[192,1,8,128]{3,2,1,0:T(8,128)(2,1)}, bf16[192,1,8,128]{3,2,1,0:T(8,128)(2,1)}, u32[]{:S(2)}, u32[]{:S(2)}) collective-permute-start(bf16[192,1,8,128]{3,2,1,0:T(8,128)(2,1)} %get-tuple-element.57), channel_id=1, source_target_pairs={{0,1},{1,2},{2,3},{3,4},{4,5},{5,6},{6,7},{7,8},{8,9},{9,10},{10,1... | collective-permute-start | bytes 1179656 | tf_op jit(solution)/shard_map/ppermute | solution.py:24
  142.0 102.1 %copy-start.3 = (bf16[96,4,8,128]{3,2,1,0:T(8,128)(2,1)S(1)}, bf16[96,4,8,128]{3,2,1,0:T(8,128)(2,1)}, u32[]{:S(2)}) copy-start(bf16[96,4,8,128]{3,2,1,0:T(8,128)(2,1)} %copy-done.2) | copy-start | bytes 2359300
  142.0 102.1 %copy-start.11 = (bf16[96,1,4,8,128]{4,3,2,1,0:T(8,128)(2,1)S(1)}, bf16[96,1,4,8,128]{4,3,2,1,0:T(8,128)(2,1)}, u32[]{:S(2)}) copy-start(bf16[96,1,4,8,128]{4,3,2,1,0:T(8,128)(2,1)} %param.9) | copy-start | bytes 2359300
  146.6 146.7 %all-to-all-start.1 = ((bf16[192,16,128]{2,0,1:T(8,128)(2,1)}), bf16[192,16,128]{2,0,1:T(8,128)(2,1)}, u32[]{:S(2)}, u32[]{:S(2)}) async-start(bf16[192,16,128]{2,0,1:T(8,128)(2,1)} %broadcast_select_fusion), calls=%async_computation.1 | async-start | bytes 1572864 | tf_op jit(solution)/shard_map/all_to_all | solution.py:119
  153.2 187.0 %all-reduce.17.cloned.1.call-start = ((), (), s32[]{:S(2)}) async-start(), calls=%async_computation.3 | async-start | bytes 491520 | tf_op jit(solution)/shard_map/psum | solution.py:171
  243.6 17.0 %copy-start.24 = (f32[4,8,128]{2,1,0:T(8,128)S(1)}, f32[4,8,128]{2,1,0:T(8,128)}, u32[]{:S(2)}) copy-start(f32[4,8,128]{2,1,0:T(8,128)} %copy-done.23) | copy-start | bytes 49156
  243.6 17.0 %copy-start.26 = (f32[4,8,128]{2,1,0:T(8,128)S(1)}, f32[4,8,128]{2,1,0:T(8,128)}, u32[]{:S(2)}) copy-start(f32[4,8,128]{2,1,0:T(8,128)} %copy-done.25) | copy-start | bytes 49156
  243.6 17.0 %copy-start.28 = (f32[4,8,128]{2,1,0:T(8,128)S(1)}, f32[4,8,128]{2,1,0:T(8,128)}, u32[]{:S(2)}) copy-start(f32[4,8,128]{2,1,0:T(8,128)} %copy-done.27) | copy-start | bytes 49156
  243.7 17.0 %copy-start.30 = (f32[4,8,128]{2,1,0:T(8,128)S(1)}, f32[4,8,128]{2,1,0:T(8,128)}, u32[]{:S(2)}) copy-start(f32[4,8,128]{2,1,0:T(8,128)} %copy-done.29) | copy-start | bytes 49156
  243.7 17.0 %copy-start.32 = (f32[4,8,128]{2,1,0:T(8,128)S(1)}, f32[4,8,128]{2,1,0:T(8,128)}, u32[]{:S(2)}) copy-start(f32[4,8,128]{2,1,0:T(8,128)} %copy-done.31) | copy-start | bytes 49156
  243.7 17.0 %copy-start.34 = (f32[4,8,128]{2,1,0:T(8,128)S(1)}, f32[4,8,128]{2,1,0:T(8,128)}, u32[]{:S(2)}) copy-start(f32[4,8,128]{2,1,0:T(8,128)} %copy-done.33) | copy-start | bytes 49156
  243.7 17.0 %copy-start.36 = (f32[4,8,128]{2,1,0:T(8,128)S(1)}, f32[4,8,128]{2,1,0:T(8,128)}, u32[]{:S(2)}) copy-start(f32[4,8,128]{2,1,0:T(8,128)} %copy-done.35) | copy-start | bytes 49156
  243.7 17.0 %copy-start.38 = (f32[4,8,128]{2,1,0:T(8,128)S(1)}, f32[4,8,128]{2,1,0:T(8,128)}, u32[]{:S(2)}) copy-start(f32[4,8,128]{2,1,0:T(8,128)} %copy-done.37) | copy-start | bytes 49156
  243.7 17.0 %copy-start.40 = (f32[4,8,128]{2,1,0:T(8,128)S(1)}, f32[4,8,128]{2,1,0:T(8,128)}, u32[]{:S(2)}) copy-start(f32[4,8,128]{2,1,0:T(8,128)} %copy-done.39) | copy-start | bytes 49156
  243.7 17.0 %copy-start.42 = (f32[4,8,128]{2,1,0:T(8,128)S(1)}, f32[4,8,128]{2,1,0:T(8,128)}, u32[]{:S(2)}) copy-start(f32[4,8,128]{2,1,0:T(8,128)} %copy-done.41) | copy-start | bytes 49156
  243.7 17.0 %copy-start.44 = (f32[4,8,128]{2,1,0:T(8,128)S(1)}, f32[4,8,128]{2,1,0:T(8,128)}, u32[]{:S(2)}) copy-start(f32[4,8,128]{2,1,0:T(8,128)} %copy-done.43) | copy-start | bytes 49156
  243.7 17.0 %copy-start.46 = (f32[4,8,128]{2,1,0:T(8,128)S(1)}, f32[4,8,128]{2,1,0:T(8,128)}, u32[]{:S(2)}) copy-start(f32[4,8,128]{2,1,0:T(8,128)} %copy-done.45) | copy-start | bytes 49156
  243.7 17.0 %copy-start.48 = (f32[4,8,128]{2,1,0:T(8,128)S(1)}, f32[4,8,128]{2,1,0:T(8,128)}, u32[]{:S(2)}) copy-start(f32[4,8,128]{2,1,0:T(8,128)} %copy-done.47) | copy-start | bytes 49156
  243.8 17.0 %copy-start.50 = (f32[4,8,128]{2,1,0:T(8,128)S(1)}, f32[4,8,128]{2,1,0:T(8,128)}, u32[]{:S(2)}) copy-start(f32[4,8,128]{2,1,0:T(8,128)} %copy-done.49) | copy-start | bytes 49156
  243.8 17.0 %copy-start.52 = (f32[4,8,128]{2,1,0:T(8,128)S(1)}, f32[4,8,128]{2,1,0:T(8,128)}, u32[]{:S(2)}) copy-start(f32[4,8,128]{2,1,0:T(8,128)} %copy-done.51) | copy-start | bytes 49156
  243.8 17.0 %copy-start.54 = (f32[4,8,128]{2,1,0:T(8,128)S(1)}, f32[4,8,128]{2,1,0:T(8,128)}, u32[]{:S(2)}) copy-start(f32[4,8,128]{2,1,0:T(8,128)} %copy-done.53) | copy-start | bytes 49156
  243.8 17.0 %copy-start.56 = (f32[4,8,128]{2,1,0:T(8,128)S(1)}, f32[4,8,128]{2,1,0:T(8,128)}, u32[]{:S(2)}) copy-start(f32[4,8,128]{2,1,0:T(8,128)} %copy-done.55) | copy-start | bytes 49156
  243.8 17.0 %copy-start.58 = (f32[4,8,128]{2,1,0:T(8,128)S(1)}, f32[4,8,128]{2,1,0:T(8,128)}, u32[]{:S(2)}) copy-start(f32[4,8,128]{2,1,0:T(8,128)} %copy-done.57) | copy-start | bytes 49156
  243.8 17.0 %copy-start.60 = (f32[4,8,128]{2,1,0:T(8,128)S(1)}, f32[4,8,128]{2,1,0:T(8,128)}, u32[]{:S(2)}) copy-start(f32[4,8,128]{2,1,0:T(8,128)} %copy-done.59) | copy-start | bytes 49156
  243.8 17.0 %copy-start.62 = (f32[4,8,128]{2,1,0:T(8,128)S(1)}, f32[4,8,128]{2,1,0:T(8,128)}, u32[]{:S(2)}) copy-start(f32[4,8,128]{2,1,0:T(8,128)} %copy-done.61) | copy-start | bytes 49156
  243.8 17.0 %copy-start.64 = (f32[4,8,128]{2,1,0:T(8,128)S(1)}, f32[4,8,128]{2,1,0:T(8,128)}, u32[]{:S(2)}) copy-start(f32[4,8,128]{2,1,0:T(8,128)} %copy-done.63) | copy-start | bytes 49156
  243.8 17.0 %copy-start.66 = (f32[4,8,128]{2,1,0:T(8,128)S(1)}, f32[4,8,128]{2,1,0:T(8,128)}, u32[]{:S(2)}) copy-start(f32[4,8,128]{2,1,0:T(8,128)} %copy-done.65) | copy-start | bytes 49156
  243.8 17.0 %copy-start.68 = (f32[4,8,128]{2,1,0:T(8,128)S(1)}, f32[4,8,128]{2,1,0:T(8,128)}, u32[]{:S(2)}) copy-start(f32[4,8,128]{2,1,0:T(8,128)} %copy-done.67) | copy-start | bytes 49156
  243.9 17.0 %copy-start.70 = (f32[4,8,128]{2,1,0:T(8,128)S(1)}, f32[4,8,128]{2,1,0:T(8,128)}, u32[]{:S(2)}) copy-start(f32[4,8,128]{2,1,0:T(8,128)} %copy-done.69) | copy-start | bytes 49156
  243.9 17.0 %copy-start.72 = (f32[4,8,128]{2,1,0:T(8,128)S(1)}, f32[4,8,128]{2,1,0:T(8,128)}, u32[]{:S(2)}) copy-start(f32[4,8,128]{2,1,0:T(8,128)} %copy-done.71) | copy-start | bytes 49156
  243.9 17.0 %copy-start.74 = (f32[4,8,128]{2,1,0:T(8,128)S(1)}, f32[4,8,128]{2,1,0:T(8,128)}, u32[]{:S(2)}) copy-start(f32[4,8,128]{2,1,0:T(8,128)} %copy-done.73) | copy-start | bytes 49156
  243.9 207.3 %all-reduce.19.cloned.1.call-start = ((), (), s32[]{:S(2)}) async-start(), calls=%async_computation.4 | async-start | bytes 589824 | tf_op jit(solution)/shard_map/psum | solution.py:174
  320.2 23.5 %copy-start.83 = (s32[288]{0:T(512)S(1)}, s32[288]{0:T(512)}, u32[]{:S(2)}) copy-start(s32[288]{0:T(512)} %iota_add_fusion) | copy-start | bytes 3460
  343.1 203.7 %all-reduce.21.cloned.1.call-start = ((), (), s32[]{:S(2)}) async-start(), calls=%async_computation.5 | async-start | bytes 589824 | tf_op jit(solution)/shard_map/psum | solution.py:174
  344.1 51.1 %copy-start.87 = (s32[2]{0:T(128)S(1)}, s32[2]{0:T(128)}, u32[]{:S(2)}) copy-start(s32[2]{0:T(128)} %iota_multiply_fusion) | copy-start | bytes 28
  344.1 51.2 %copy-start.76 = (f32[2,128,128]{2,1,0:T(8,128)S(1)}, f32[2,128,128]{2,1,0:T(8,128)}, u32[]{:S(2)}) copy-start(f32[2,128,128]{2,1,0:T(8,128)} %custom-call.29) | copy-start | bytes 393220
  344.1 55.0 %copy-start.20 = (f32[128,96]{1,0:T(8,128)S(1)}, f32[128,96]{1,0:T(8,128)}, u32[]{:S(2)}) copy-start(f32[128,96]{1,0:T(8,128)} %pad_convert_fusion) | copy-start | bytes 147460
  356.0 73.8 %copy-start.17 = (f32[288,288]{0,1:T(8,128)S(1)}, f32[288,288]{0,1:T(8,128)}, u32[]{:S(2)}) copy-start(f32[288,288]{0,1:T(8,128)} %fusion.57) | copy-start | bytes 995332
  (34 other events, 224.9 us)
Sparse Core Ops, SparseCore 0:
  132.4 111.1 all-reduce.14
  246.8 93.3 all-reduce.16
  343.2 107.8 all-reduce.18
  454.3 92.5 all-reduce.20
